TPU v7x, 32 devices: a whole 2x2x4 slice. The times are simulated.
32 devices in a mesh: seq: 8 (over z, x), tp: 4 (over y, core).
Axes of the slice: x: 2, y: 2, z: 4, core: 2. Of those that a mesh axis runs over, the one named last changes fastest.
Arguments:
- query_in: bfloat16 [4096, 4096], P('seq', 'tp'), may hold values from -6 to 6
- key_in: bfloat16 [4096, 4096], P('seq', 'tp'), may hold values from -6 to 6
- value_in: bfloat16 [4096, 4096], P('seq', 'tp'), may hold values from -6 to 6
- feature_taps: float32 [7, 3, 4096], P(None, None, 'tp'), may hold values from -2 to 2
- filter_taps: bfloat16 [256, 128], P('tp'), may hold values from -0.5 to 0.5
- out_weight: bfloat16 [4096, 4096], P('tp'), may hold values from -0.09375 to 0.09375
- cotangent: bfloat16 [4096, 4096], P(('seq', 'tp')), may hold values from -6 to 6
Outputs:
- block_out: bfloat16 [4096, 4096], P(('seq', 'tp'))
- query_grad: bfloat16 [4096, 4096], P('seq', 'tp')
- key_grad: bfloat16 [4096, 4096], P('seq', 'tp')
- value_grad: bfloat16 [4096, 4096], P('seq', 'tp')
- weight_grad: bfloat16 [4096, 4096], P('tp', 'seq')
All inputs are finite; a program needn't handle non-finite values.
Results may differ from a plain program's by a relative error of at most 0.012.
Values may be sent and summed in bfloat16 or wider, within the bound.
No kernel may reach another device: no remote copies, remote signals or barrier semaphores. Data moves between devices by JAX's collectives and lax.ppermute only.
A program may use at most 128 MiB of HBM per device.

v0:
```python
import jax
import jax.numpy as jnp
from jax import lax
from jax.sharding import PartitionSpec as P


def passed_along(value, axis, steps):
    count = lax.axis_size(axis)
    leading, last = (max(0, -steps), min(count, count - steps))
    return lax.ppermute(value, axis, [(source, source + steps) for source in range(leading, last)])


def featurize(extended, feature_taps, out_rows):
    tap_span = feature_taps.shape[0]
    summed = jnp.zeros((out_rows,) + extended.shape[1:], jnp.float32)
    for offset in range(tap_span):
        first_row = tap_span - 1 - offset
        summed = summed + feature_taps[offset] * extended[first_row : first_row + out_rows].astype(
            jnp.float32
        )
    return summed


def spread_back(extended, feature_taps, out_rows):
    tap_span = feature_taps.shape[0]
    summed = jnp.zeros((out_rows,) + extended.shape[1:], jnp.float32)
    for offset in range(tap_span):
        summed = summed + feature_taps[offset] * extended[offset : offset + out_rows]
    return summed


def band_table(filter_taps):
    tap_count = filter_taps.shape[1]
    window_rows = 2 * tap_count
    lag_index = jnp.arange(tap_count)[:, None, None]
    row_index = jnp.arange(window_rows)[None, :, None]
    col_index = jnp.arange(tap_count)[None, None, :]
    select = (col_index + tap_count - row_index == lag_index).astype(jnp.bfloat16)
    select = select.reshape(tap_count, window_rows * tap_count)
    toeplitz_table = jnp.dot(filter_taps, select, preferred_element_type=jnp.float32)
    return toeplitz_table.astype(jnp.bfloat16).reshape(filter_taps.shape[0], window_rows, tap_count)


def band_mix(padded_rows, toeplitz_table):
    group_count, window_rows, tap_count = toeplitz_table.shape
    row_count = padded_rows.shape[0] - tap_count
    block_count = row_count // tap_count
    channels = padded_rows.shape[1]
    lower_half = padded_rows[:row_count].reshape(block_count, tap_count, channels)
    upper_half = padded_rows[tap_count:].reshape(block_count, tap_count, channels)
    window = jnp.concatenate([lower_half, upper_half], axis=1)
    window = window.reshape(block_count, window_rows, group_count, channels // group_count)
    mixed_rows = jnp.einsum(
        "nwgc,gwt->ntgc", window, toeplitz_table, preferred_element_type=jnp.float32
    )
    return mixed_rows.reshape(row_count, channels)


def per_device(query_in, key_in, value_in, feature_taps, filter_taps, out_weight, cotangent):
    row_count, channels = query_in.shape
    tap_count = filter_taps.shape[1]
    tap_span = feature_taps.shape[0]
    stacked = jnp.stack([query_in, key_in, value_in], axis=1)
    before = passed_along(stacked[row_count - tap_span + 1 :], "seq", 1)
    features = featurize(jnp.concatenate([before, stacked], axis=0), feature_taps, row_count)
    mix_rows = (features[:, 1] * features[:, 2]).astype(jnp.bfloat16)
    mix_before = passed_along(mix_rows[row_count - tap_count :], "seq", 1)
    padded_mix = jnp.concatenate([mix_before, mix_rows], axis=0)
    query_feat = features[:, 0]
    key_feat = features[:, 1]
    value_feat = features[:, 2]
    toeplitz_rows = band_table(filter_taps)
    long_conv = band_mix(padded_mix, toeplitz_rows)
    gated_rows = (query_feat * long_conv).astype(jnp.bfloat16)
    block_out = lax.psum_scatter(
        jnp.dot(gated_rows, out_weight, preferred_element_type=jnp.float32).astype(jnp.bfloat16),
        "tp",
        scatter_dimension=0,
        tiled=True,
    )
    full_cotangent = lax.all_gather(cotangent, "tp", axis=0, tiled=True)
    grad_gated = lax.dot_general(
        full_cotangent, out_weight, (((1,), (1,)), ((), ())), preferred_element_type=jnp.float32
    )
    grad_conv = (grad_gated * query_feat).astype(jnp.bfloat16)
    grad_query = grad_gated * long_conv
    conv_after = passed_along(grad_conv[:tap_count], "seq", -1)
    grad_mix = band_mix(
        jnp.concatenate([grad_conv, conv_after], axis=0), toeplitz_rows[:, ::-1, ::-1]
    )
    grad_features = jnp.stack([grad_query, grad_mix * value_feat, grad_mix * key_feat], axis=1)
    features_after = passed_along(
        grad_features[: tap_span - 1].astype(jnp.bfloat16), "seq", -1
    ).astype(jnp.float32)
    grad_inputs = spread_back(
        jnp.concatenate([grad_features, features_after], axis=0), feature_taps, row_count
    ).astype(jnp.bfloat16)
    seq_count = lax.axis_size("seq")
    grad_scale = (row_count * seq_count) ** (-0.5)
    local_grad = (
        lax.dot_general(
            gated_rows, full_cotangent, (((0,), (0,)), ((), ())), preferred_element_type=jnp.float32
        )
        * grad_scale
    )
    summed_grad = lax.psum_scatter(
        local_grad.astype(jnp.bfloat16), "seq", scatter_dimension=1, tiled=True
    )
    return (block_out, grad_inputs[:, 0], grad_inputs[:, 1], grad_inputs[:, 2], summed_grad)


def solution(mesh):
    placed = (
        P("seq", "tp"),
        P("seq", "tp"),
        P("seq", "tp"),
        P(None, None, "tp"),
        P("tp", None),
        P("tp", None),
        P(("seq", "tp"), None),
    )
    return jax.shard_map(
        per_device,
        mesh=mesh,
        in_specs=placed,
        out_specs=(
            P(("seq", "tp"), None),
            P("seq", "tp"),
            P("seq", "tp"),
            P("seq", "tp"),
            P("tp", "seq"),
        ),
        check_vma=False,
    )
```

profile of v0, /device:TPU:0, one launch (start us, length us, event | category | flops | bytes accessed | tf_op | source)
XLA Modules:
  0.0 389.7 jit_solution(14362867363765018553)
XLA Ops:
  7.3 0.7 all-gather.2.cloned.1.call-update
  8.0 2.4 pad_maximum_fusion.2
  10.4 4.9 %collective-permute-start = (bf16[6,3,1024]{2,0,1:T(8,128)(2,1)S(1)}, bf16[6,3,1024]{2,0,1:T(8,128)(2,1)S(1)}, u32[]{:S(2)}, u32[]{:S(2)}) collective-permute-start(bf16[6,3,1024]{2,0,1:T(8,128)(2,1)S(1)} %slice.138), channel_id=1, source_target_pairs={{0,4},{4,8},{8,12},{12,16},{16,20},{20,24},{24,28},{1,5},{5,9},{9,... | collective-permute-start | bytes 110600 | tf_op jit(solution)/shard_map/ppermute | solution.py:10
  15.4 1.6 collective-permute-done
  17.0 1.1 maximum_maximum_fusion
  18.1 6.4 %multiply_add_fusion = f32[512,3,1024]{2,0,1:T(8,128)} fusion(bf16[518,3,1024]{2,0,1:T(8,128)(2,1)S(1)} %maximum_maximum_fusion, f32[3,1024]{1,0:T(4,128)S(1)} %get-tuple-element.22, f32[3,1024]{1,0:T(4,128)S(1)} %get-tuple-element.23, f32[3,1024]{1,0:T(4,128)S(1)} %get-tuple-element.24, f32[3,1024]{1,0:T(4,128)S(1)} %get-tuple-element.25, ...), kind=kLoop, calls=%fused_computation.19 | loop fusion | flops 34603008 | bytes 28397568 | tf_op jit(solution)/shard_map/add | solution.py:18
  24.5 22.3 %all-gather.2.cloned.1.call-done = bf16[512,4096]{1,0:T(8,128)(2,1)} async-done(((bf16[128,4096]{1,0:T(8,128)(2,1)}), bf16[512,4096]{1,0:T(8,128)(2,1)}) %all-gather.2.cloned.1.call-update) | async-done | bytes 4194320 | tf_op jit(solution)/shard_map/all_gather | solution.py:81
  46.8 11.1 %multiply_convert_fusion.1 = (bf16[512,1024]{1,0:T(8,128)(2,1)S(1)}, f32[512,1024]{1,0:T(8,128)}) fusion(f32[512,3,1024]{2,0,1:T(8,128)} %multiply_add_fusion, bf16[512,4096]{1,0:T(8,128)(2,1)} %all-gather.2.cloned.1.call-done, bf16[1024,4096]{1,0:T(8,128)(2,1)} %param.12), kind=kOutput, calls=%fused_computation.28 | convolution fusion | flops 4296015872 | bytes 17825792 | tf_op jit(solution)/shard_map/dot_general | solution.py:82
  57.9 0.7 slice.149
  58.6 1.5 collective-permute-start.2
  60.1 3.9 fusion.8
  64.0 3.1 copy.36
  67.1 62.5 %rev.3 = bf16[64,256,128]{2,1,0:T(8,128)(2,1)} reverse(bf16[64,256,128]{2,1,0:T(8,128)(2,1)} %bitcast.81), dimensions={1,2} | reverse | bytes 8388608 | tf_op jit(solution)/shard_map/rev | solution.py:89
  129.6 0.5 copy.22
  130.2 0.3 concatenate.30
  130.8 0.5 copy.23
  132.0 0.3 pad_maximum_fusion.4
  132.3 1.6 copy-done.5
  133.9 0.9 fusion.11
  134.7 1.0 copy.26
  135.7 1.8 reshape.75
  137.6 2.9 copy.27
  140.4 5.2 %slice_multiply_fusion.6 = (f32[512,1,1024]{2,0,1:T(8,128)S(1)}, f32[512,1,1024]{2,0,1:T(8,128)}, bf16[512,1,1024]{2,0,1:T(8,128)(2,1)S(1)}) fusion(f32[512,1,1024]{2,0,1:T(8,128)} %copy.27, f32[512,3,1024]{2,0,1:T(8,128)} %multiply_add_fusion), kind=kLoop, calls=%fused_computation.32 | loop fusion | flops 2097152 | bytes 11534336 | tf_op jit(solution)/shard_map/mul | solution.py:91
  145.7 0.7 slice_bitcast_fusion.4
  146.4 4.8 %collective-permute-start.1 = (bf16[128,1024]{1,0:T(8,128)(2,1)}, bf16[128,1024]{1,0:T(8,128)(2,1)S(1)}, u32[]{:S(2)}, u32[]{:S(2)}) collective-permute-start(bf16[128,1024]{1,0:T(8,128)(2,1)} %slice_bitcast_fusion.4), channel_id=1, source_target_pairs={{0,4},{4,8},{8,12},{12,16},{16,20},{20,24},{24,28},{1,5},{5,9},{9,... | collective-permute-start | bytes 786440 | tf_op jit(solution)/shard_map/ppermute | solution.py:10
  151.2 1.3 copy.16
  152.5 2.1 convert_element_type.69
  154.6 2.5 copy.18
  157.1 1.0 pad_maximum_fusion.6
  158.1 1.5 copy.15
  159.6 1.1 concatenate.28
  160.7 1.6 copy.17
  162.4 1.6 pad_maximum_fusion.3
  163.9 0.9 fusion.10
  164.8 1.0 copy.19
  165.8 1.5 copy.46
  167.3 3.0 copy.20
  170.2 5.1 %multiply_bitcast_fusion = (f32[512,1,1024]{2,0,1:T(8,128)}, bf16[512,1024]{1,0:T(8,128)(2,1)S(1)}) fusion(f32[512,1024]{1,0:T(8,128)} %get-tuple-element.21, f32[512,1024]{1,0:T(8,128)} %copy.20, f32[512,3,1024]{2,0,1:T(8,128)} %multiply_add_fusion), kind=kLoop, calls=%fused_computation.29 | loop fusion | flops 1572864 | bytes 9437184 | tf_op jit(solution)/shard_map/stack | solution.py:91
  175.3 9.4 %convolution_convert_fusion.1 = bf16[512,4096]{1,0:T(8,128)(2,1)} fusion(bf16[512,1024]{1,0:T(8,128)(2,1)S(1)} %get-tuple-element.12, bf16[1024,4096]{1,0:T(8,128)(2,1)} %param.12), kind=kOutput, calls=%fused_computation.20 | convolution fusion | flops 4297064448 | bytes 13631488 | tf_op jit(solution)/shard_map/dot_general | solution.py:76
  184.8 9.0 %multiply_convert_fusion = bf16[1024,4096]{1,0:T(8,128)(2,1)} fusion(bf16[512,1024]{1,0:T(8,128)(2,1)S(1)} %get-tuple-element.12, bf16[512,4096]{1,0:T(8,128)(2,1)} %all-gather.2.cloned.1.call-done), kind=kOutput, calls=%fused_computation.1 | convolution fusion | flops 4303355904 | bytes 13631488 | tf_op jit(solution)/shard_map/dot_general | solution.py:101
  193.9 3.9 pad_maximum_fusion.1
  197.8 1.6 collective-permute-start.3
  199.3 4.6 %collective-permute-done.3 = bf16[6,3,1024]{2,0,1:T(8,128)(2,1)S(1)} collective-permute-done((bf16[6,3,1024]{2,0,1:T(8,128)(2,1)S(1)}, bf16[6,3,1024]{2,0,1:T(8,128)(2,1)S(1)}, u32[]{:S(2)}, u32[]{:S(2)}) %collective-permute-start.3) | collective-permute-done | bytes 36896 | tf_op jit(solution)/shard_map/ppermute | solution.py:10
  203.9 3.1 pad_maximum_fusion
  207.1 18.3 %fusion.2 = bf16[512,3,1024]{2,0,1:T(8,128)(2,1)} fusion(f32[518,3,1024]{2,0,1:T(8,128)} %pad_maximum_fusion, f32[3,1024]{1,0:T(4,128)S(1)} %get-tuple-element.22, f32[3,1024]{1,0:T(4,128)S(1)} %get-tuple-element.23, f32[3,1024]{1,0:T(4,128)S(1)} %get-tuple-element.24, f32[3,1024]{1,0:T(4,128)S(1)} %get-tuple-element.25, f32[3,1024]{1,0:T(4,128)S(1)} %get-tuple-element.26, ...), kind=kLoop, calls=%fused_computation.7 | loop fusion | flops 25165824 | bytes 47271936 | tf_op jit(solution)/shard_map/convert_element_type | solution.py:97
  225.4 3.6 slice_bitcast_fusion.1
  229.0 2.1 reduce-scatter.3.cloned.1.call-done
  231.1 152.1 %reduce-scatter.5.cloned.1.call-done = bf16[1024,512]{1,0:T(8,128)(2,1)} async-done(((bf16[1024,4096]{1,0:T(8,128)(2,1)}), bf16[1024,512]{1,0:T(8,128)(2,1)}) %reduce-scatter.5.cloned.1.call-update) | async-done | bytes 1048592 | tf_op jit(solution)/shard_map/reduce_scatter | solution.py:106
  (40 shorter events, 1.2 us)
Async XLA Ops:
  7.2 52.9 %copy-start = (bf16[64,128]{1,0:T(8,128)(2,1)S(1)}, bf16[64,128]{1,0:T(8,128)(2,1)}, u32[]{:S(2)}) copy-start(bf16[64,128]{1,0:T(8,128)(2,1)} %param.11) | copy-start | bytes 49156
  7.2 9.8 %copy-start.6 = (bf16[512,1024]{1,0:T(8,128)(2,1)S(1)}, bf16[512,1024]{1,0:T(8,128)(2,1)}, u32[]{:S(2)}) copy-start(bf16[512,1024]{1,0:T(8,128)(2,1)} %param.9) | copy-start | bytes 3145732
  7.2 9.8 %copy-start.7 = (bf16[512,1024]{1,0:T(8,128)(2,1)S(1)}, bf16[512,1024]{1,0:T(8,128)(2,1)}, u32[]{:S(2)}) copy-start(bf16[512,1024]{1,0:T(8,128)(2,1)} %param.8) | copy-start | bytes 3145732
  7.2 9.8 %copy-start.8 = (bf16[512,1024]{1,0:T(8,128)(2,1)S(1)}, bf16[512,1024]{1,0:T(8,128)(2,1)}, u32[]{:S(2)}) copy-start(bf16[512,1024]{1,0:T(8,128)(2,1)} %param.7) | copy-start | bytes 3145732
  7.2 8.1 %copy-start.9 = (f32[7,3,1024]{2,0,1:T(8,128)S(1)}, f32[7,3,1024]{2,0,1:T(8,128)}, u32[]{:S(2)}) copy-start(f32[7,3,1024]{2,0,1:T(8,128)} %param.10) | copy-start | bytes 258052
  7.2 39.6 %all-gather.2.cloned.1.call-start = ((), (), s32[]{:S(2)}) async-start(), calls=%async_computation.3 | async-start | bytes 5242880 | tf_op jit(solution)/shard_map/all_gather | solution.py:81
  8.0 223.2 %reduce-scatter.3.cloned.1.call-start = ((), (), s32[]{:S(2)}) async-start(), calls=%async_computation.2 | async-start | bytes 5242880 | tf_op jit(solution)/shard_map/reduce_scatter | solution.py:75
  10.4 6.6 %collective-permute-start = (bf16[6,3,1024]{2,0,1:T(8,128)(2,1)S(1)}, bf16[6,3,1024]{2,0,1:T(8,128)(2,1)S(1)}, u32[]{:S(2)}, u32[]{:S(2)}) collective-permute-start(bf16[6,3,1024]{2,0,1:T(8,128)(2,1)S(1)} %slice.138), channel_id=1, source_target_pairs={{0,4},{4,8},{8,12},{12,16},{16,20},{20,24},{24,28},{1,5},{5,9},{9,... | collective-permute-start | bytes 110600 | tf_op jit(solution)/shard_map/ppermute | solution.py:10
  58.6 72.1 %collective-permute-start.2 = (bf16[128,1024]{1,0:T(8,128)(2,1)}, bf16[128,1024]{1,0:T(8,128)(2,1)S(1)}, u32[]{:S(2)}, u32[]{:S(2)}) collective-permute-start(bf16[128,1024]{1,0:T(8,128)(2,1)} %slice.149), channel_id=1, source_target_pairs={{4,0},{8,4},{12,8},{16,12},{20,16},{24,20},{28,24},{5,1},{9,5},{13... | collective-permute-start | bytes 786440 | tf_op jit(solution)/shard_map/ppermute | solution.py:10
  131.7 2.2 copy-start.5
  146.4 10.7 %collective-permute-start.1 = (bf16[128,1024]{1,0:T(8,128)(2,1)}, bf16[128,1024]{1,0:T(8,128)(2,1)S(1)}, u32[]{:S(2)}, u32[]{:S(2)}) collective-permute-start(bf16[128,1024]{1,0:T(8,128)(2,1)} %slice_bitcast_fusion.4), channel_id=1, source_target_pairs={{0,4},{4,8},{8,12},{12,16},{16,20},{20,24},{24,28},{1,5},{5,9},{9,... | collective-permute-start | bytes 786440 | tf_op jit(solution)/shard_map/ppermute | solution.py:10
  160.7 3.2 copy-start.2
  184.8 198.4 %reduce-scatter.5.cloned.1.call-start = ((), (), s32[]{:S(2)}) async-start(), calls=%async_computation.4 | async-start | bytes 9437184 | tf_op jit(solution)/shard_map/reduce_scatter | solution.py:106
  193.9 10.0 %copy-start.3 = (f32[512,1,1024]{2,0,1:T(8,128)S(1)}, f32[512,1,1024]{2,0,1:T(8,128)}, u32[]{:S(2)}) copy-start(f32[512,1,1024]{2,0,1:T(8,128)} %get-tuple-element.6) | copy-start | bytes 6291460
  193.9 10.0 %copy-start.4 = (f32[512,1,1024]{2,0,1:T(8,128)S(1)}, f32[512,1,1024]{2,0,1:T(8,128)}, u32[]{:S(2)}) copy-start(f32[512,1,1024]{2,0,1:T(8,128)} %get-tuple-element.11) | copy-start | bytes 6291460
  197.8 6.1 %collective-permute-start.3 = (bf16[6,3,1024]{2,0,1:T(8,128)(2,1)S(1)}, bf16[6,3,1024]{2,0,1:T(8,128)(2,1)S(1)}, u32[]{:S(2)}, u32[]{:S(2)}) collective-permute-start(bf16[6,3,1024]{2,0,1:T(8,128)(2,1)S(1)} %slice.210), channel_id=1, source_target_pairs={{4,0},{8,4},{12,8},{16,12},{20,16},{24,20},{28,24},{5,1},{9,5},{13... | collective-permute-start | bytes 110600 | tf_op jit(solution)/shard_map/ppermute | solution.py:10
  207.1 176.1 %copy-start.1 = (bf16[64,128]{1,0:T(8,128)(2,1)S(1)}, bf16[64,128]{1,0:T(8,128)(2,1)}, u32[]{:S(2)}) copy-start(bf16[64,128]{1,0:T(8,128)(2,1)} %param.11) | copy-start | bytes 49156
Sparse Core Ops, SparseCore 0:
  9.6 37.1 all-gather.1
  184.9 46.1 reduce-scatter.2
  235.3 147.8 reduce-scatter.4
where the time goes:
time: 397 us; the launch traced here: 390 us
  waiting for transfers between devices  183 us (46%)
  local copies, waits for them, and re-layouts  95.8 us (24%)
  other arithmetic  48.5 us (12%)
  matrix products  35.1 us (9%)
  between operations  14.1 us (4%)
  starting transfers between devices  12.8 us (3%)
    reduce_scatter x1, waiting for transfers between devices, per_device(): lax.psum_scatter(local_grad.astype(jnp.bfloat16), 'seq', scatter_dimensio...  152 us
    rev x1, local copies, waits for them, and re-layouts, per_device(): toeplitz_rows[:, ::-1, ::-1]  62.5 us
    all_gather x1, waiting for transfers between devices, per_device(): full_cotangent = lax.all_gather(cotangent, 'tp', axis=0, tiled=True)  22.3 us
    convert_element_type x1, other arithmetic, per_device(): grad_inputs = spread_back(jnp.concatenate([grad_features, features_after]...  18.3 us
    ppermute x4, starting transfers between devices, passed_along(): lax.ppermute(value, axis, [(source, source + steps) for source in range(l...  12.7 us
    dot_general x1, matrix products, per_device(): lax.dot_general(full_cotangent, out_weight, (((1,), (1,)), ((), ())), pre...  11.1 us
    dot_general x1, matrix products, per_device(): jnp.dot(gated_rows, out_weight, preferred_element_type=jnp.float32)  9.41 us
    dot_general x1, matrix products, per_device(): lax.dot_general(gated_rows, full_cotangent, (((0,), (0,)), ((), ())), pre...  9.01 us
  transfers between devices with their start and end apart: 7, of which 5 were waited for; matrix products, arithmetic and copies ran while one was open for 32% of the time, Pallas kernels for 0%

commit v1 on v0

--- a/solution.py
+++ b/solution.py
@@ -29,13 +29,16 @@
     return summed
 
 
-def band_table(filter_taps):
+def band_table(filter_taps, reverse=False):
     tap_count = filter_taps.shape[1]
     window_rows = 2 * tap_count
     lag_index = jnp.arange(tap_count)[:, None, None]
     row_index = jnp.arange(window_rows)[None, :, None]
     col_index = jnp.arange(tap_count)[None, None, :]
-    select = (col_index + tap_count - row_index == lag_index).astype(jnp.bfloat16)
+    if reverse:
+        select = (row_index - col_index == lag_index).astype(jnp.bfloat16)
+    else:
+        select = (col_index + tap_count - row_index == lag_index).astype(jnp.bfloat16)
     select = select.reshape(tap_count, window_rows * tap_count)
     toeplitz_table = jnp.dot(filter_taps, select, preferred_element_type=jnp.float32)
     return toeplitz_table.astype(jnp.bfloat16).reshape(filter_taps.shape[0], window_rows, tap_count)
@@ -86,7 +89,7 @@
     grad_query = grad_gated * long_conv
     conv_after = passed_along(grad_conv[:tap_count], "seq", -1)
     grad_mix = band_mix(
-        jnp.concatenate([grad_conv, conv_after], axis=0), toeplitz_rows[:, ::-1, ::-1]
+        jnp.concatenate([grad_conv, conv_after], axis=0), band_table(filter_taps, reverse=True)
     )
     grad_features = jnp.stack([grad_query, grad_mix * value_feat, grad_mix * key_feat], axis=1)
     features_after = passed_along(

time: 397 us -> 333 us (0.84); the launches traced: 390 us -> 333 us
  local copies, waits for them, and re-layouts: 95.8 us -> 36.3 us
  matrix products: 35.1 us -> 39.1 us
    rev x1 -> x0, local copies, waits for them, and re-layouts: 62.5 us -> none  [per_device(): toeplitz_rows[:, ::-1, ::-1]]
    unnamed x26 -> x29, local copies, waits for them, and re-layouts: 6.24 us -> 9.33 us
  transfers between devices with their start and end apart: 7 -> 7, of which waited for: 5 -> 6; matrix products, arithmetic and copies ran while one was open for 32% -> 21% of each run, Pallas kernels for 0% -> 0%
where the time goes in v1:
time: 333 us
  waiting for transfers between devices  182 us (55%)
  other arithmetic  48.4 us (15%)
  matrix products  39.1 us (12%)
  local copies, waits for them, and re-layouts  36.3 us (11%)
  between operations  14.1 us (4%)
  starting transfers between devices  12.5 us (4%)
    reduce_scatter x1, waiting for transfers between devices, per_device(): lax.psum_scatter(local_grad.astype(jnp.bfloat16), 'seq', scatter_dimensio...  152 us
    all_gather x1, waiting for transfers between devices, per_device(): full_cotangent = lax.all_gather(cotangent, 'tp', axis=0, tiled=True)  22.3 us
    convert_element_type x1, other arithmetic, per_device(): grad_inputs = spread_back(jnp.concatenate([grad_features, features_after]...  18.3 us
    ppermute x4, starting transfers between devices, passed_along(): lax.ppermute(value, axis, [(source, source + steps) for source in range(l...  12.1 us
    dot_general x1, matrix products, per_device(): lax.dot_general(full_cotangent, out_weight, (((1,), (1,)), ((), ())), pre...  11.1 us
    dot_general x1, matrix products, per_device(): jnp.dot(gated_rows, out_weight, preferred_element_type=jnp.float32)  9.42 us
    unnamed x29, local copies, waits for them, and re-layouts  9.33 us
    dot_general x1, matrix products, per_device(): lax.dot_general(gated_rows, full_cotangent, (((0,), (0,)), ((), ())), pre...  9.13 us
  transfers between devices with their start and end apart: 7, of which 6 were waited for; matrix products, arithmetic and copies ran while one was open for 21% of the time, Pallas kernels for 0%

profile of v1, /device:TPU:0, one launch (start us, length us, event | category | flops | bytes accessed | tf_op | source)
XLA Modules:
  0.0 332.6 jit_solution(7465381158730597024)
XLA Ops:
  7.3 0.7 all-gather.2.cloned.1.call-update
  8.0 2.4 pad_maximum_fusion.2
  10.4 4.9 %collective-permute-start = (bf16[6,3,1024]{2,0,1:T(8,128)(2,1)S(1)}, bf16[6,3,1024]{2,0,1:T(8,128)(2,1)S(1)}, u32[]{:S(2)}, u32[]{:S(2)}) collective-permute-start(bf16[6,3,1024]{2,0,1:T(8,128)(2,1)S(1)} %slice.138), channel_id=1, source_target_pairs={{0,4},{4,8},{8,12},{12,16},{16,20},{20,24},{24,28},{1,5},{5,9},{9,... | collective-permute-start | bytes 110600 | tf_op jit(solution)/shard_map/ppermute | solution.py:10
  15.4 0.7 subtract_bitcast_fusion
  16.1 0.9 collective-permute-done
  17.0 1.1 maximum_maximum_fusion
  18.1 6.4 %multiply_add_fusion = f32[512,3,1024]{2,0,1:T(8,128)} fusion(bf16[518,3,1024]{2,0,1:T(8,128)(2,1)S(1)} %maximum_maximum_fusion, f32[3,1024]{1,0:T(4,128)S(1)} %get-tuple-element.22, f32[3,1024]{1,0:T(4,128)S(1)} %get-tuple-element.23, f32[3,1024]{1,0:T(4,128)S(1)} %get-tuple-element.24, f32[3,1024]{1,0:T(4,128)S(1)} %get-tuple-element.25, ...), kind=kLoop, calls=%fused_computation.22 | loop fusion | flops 34603008 | bytes 28397568 | tf_op jit(solution)/shard_map/add | solution.py:18
  24.5 22.3 %all-gather.2.cloned.1.call-done = bf16[512,4096]{1,0:T(8,128)(2,1)} async-done(((bf16[128,4096]{1,0:T(8,128)(2,1)}), bf16[512,4096]{1,0:T(8,128)(2,1)}) %all-gather.2.cloned.1.call-update) | async-done | bytes 4194320 | tf_op jit(solution)/shard_map/all_gather | solution.py:84
  46.8 11.1 %multiply_convert_fusion.1 = (bf16[512,1024]{1,0:T(8,128)(2,1)S(1)}, f32[512,1024]{1,0:T(8,128)}) fusion(f32[512,3,1024]{2,0,1:T(8,128)} %multiply_add_fusion, bf16[512,4096]{1,0:T(8,128)(2,1)} %all-gather.2.cloned.1.call-done, bf16[1024,4096]{1,0:T(8,128)(2,1)} %param.12), kind=kOutput, calls=%fused_computation.32 | convolution fusion | flops 4296015872 | bytes 17825792 | tf_op jit(solution)/shard_map/dot_general | solution.py:85
  57.9 0.7 slice.149
  58.6 1.5 collective-permute-start.2
  60.1 3.9 %fusion.10 = bf16[8,8,256,128]{3,1,2,0:T(8,128)(2,1)S(1)} fusion(bf16[64,128]{1,0:T(8,128)(2,1)S(1)} %copy-done, s32[32768]{0:T(1024)S(1)} %copy-done.9), kind=kOutput, calls=%fused_computation.27 | convolution fusion | flops 543162368 | bytes 4341760 | tf_op jit(solution)/shard_map/dot_general | solution.py:43
  64.0 3.1 copy.38
  67.1 0.5 copy.22
  68.2 1.0 collective-permute-done.2
  69.2 0.5 copy.23
  70.7 1.6 copy-done.4
  72.3 0.9 fusion.13
  73.1 1.0 copy.26
  74.1 1.9 reshape.98
  76.0 2.9 copy.27
  78.8 5.2 %slice_multiply_fusion.6 = (f32[512,1,1024]{2,0,1:T(8,128)S(1)}, f32[512,1,1024]{2,0,1:T(8,128)}, bf16[512,1,1024]{2,0,1:T(8,128)(2,1)S(1)}) fusion(f32[512,1,1024]{2,0,1:T(8,128)} %copy.27, f32[512,3,1024]{2,0,1:T(8,128)} %multiply_add_fusion), kind=kLoop, calls=%fused_computation.36 | loop fusion | flops 2097152 | bytes 11534336 | tf_op jit(solution)/shard_map/mul | solution.py:94
  84.1 0.7 slice_bitcast_fusion.4
  84.8 4.5 %collective-permute-start.1 = (bf16[128,1024]{1,0:T(8,128)(2,1)}, bf16[128,1024]{1,0:T(8,128)(2,1)S(1)}, u32[]{:S(2)}, u32[]{:S(2)}) collective-permute-start(bf16[128,1024]{1,0:T(8,128)(2,1)} %slice_bitcast_fusion.4), channel_id=1, source_target_pairs={{0,4},{4,8},{8,12},{12,16},{16,20},{20,24},{24,28},{1,5},{5,9},{9,... | collective-permute-start | bytes 786440 | tf_op jit(solution)/shard_map/ppermute | solution.py:10
  89.3 3.9 %fusion.9 = bf16[8,8,256,128]{3,1,2,0:T(8,128)(2,1)S(1)} fusion(bf16[64,128]{1,0:T(8,128)(2,1)S(1)} %copy-done, s32[32768]{0:T(1024)S(1)} %subtract_bitcast_fusion.1), kind=kOutput, calls=%fused_computation.26 | convolution fusion | flops 543162368 | bytes 4341760 | tf_op jit(solution)/shard_map/dot_general | solution.py:43
  93.2 3.1 copy.36
  96.3 1.3 copy.16
  97.6 2.1 convert_element_type.76
  99.7 2.5 copy.18
  102.2 1.0 pad_maximum_fusion.6
  103.2 1.5 copy.15
  104.7 1.1 concatenate.28
  105.9 1.6 copy.17
  107.5 1.6 pad_maximum_fusion.3
  109.1 0.9 fusion.12
  109.9 1.0 copy.19
  110.9 1.5 copy.47
  112.4 3.0 copy.20
  115.3 5.1 %multiply_bitcast_fusion = (f32[512,1,1024]{2,0,1:T(8,128)}, bf16[512,1024]{1,0:T(8,128)(2,1)S(1)}) fusion(f32[512,1024]{1,0:T(8,128)} %get-tuple-element.21, f32[512,1024]{1,0:T(8,128)} %copy.20, f32[512,3,1024]{2,0,1:T(8,128)} %multiply_add_fusion), kind=kLoop, calls=%fused_computation.33 | loop fusion | flops 1572864 | bytes 9437184 | tf_op jit(solution)/shard_map/stack | solution.py:94
  120.4 9.4 %convolution_convert_fusion.2 = bf16[512,4096]{1,0:T(8,128)(2,1)} fusion(bf16[512,1024]{1,0:T(8,128)(2,1)S(1)} %get-tuple-element.12, bf16[1024,4096]{1,0:T(8,128)(2,1)} %param.12), kind=kOutput, calls=%fused_computation.23 | convolution fusion | flops 4297064448 | bytes 13631488 | tf_op jit(solution)/shard_map/dot_general | solution.py:79
  130.2 9.1 %multiply_convert_fusion = bf16[1024,4096]{1,0:T(8,128)(2,1)} fusion(bf16[512,1024]{1,0:T(8,128)(2,1)S(1)} %get-tuple-element.12, bf16[512,4096]{1,0:T(8,128)(2,1)} %all-gather.2.cloned.1.call-done), kind=kOutput, calls=%fused_computation.2 | convolution fusion | flops 4303355904 | bytes 13631488 | tf_op jit(solution)/shard_map/dot_general | solution.py:104
  139.4 3.1 pad_maximum_fusion.1
  142.5 1.3 collective-permute-start.3
  143.8 4.7 %collective-permute-done.3 = bf16[6,3,1024]{2,0,1:T(8,128)(2,1)S(1)} collective-permute-done((bf16[6,3,1024]{2,0,1:T(8,128)(2,1)S(1)}, bf16[6,3,1024]{2,0,1:T(8,128)(2,1)S(1)}, u32[]{:S(2)}, u32[]{:S(2)}) %collective-permute-start.3) | collective-permute-done | bytes 36896 | tf_op jit(solution)/shard_map/ppermute | solution.py:10
  148.6 3.1 pad_maximum_fusion
  151.7 18.3 %fusion.3 = bf16[512,3,1024]{2,0,1:T(8,128)(2,1)} fusion(f32[518,3,1024]{2,0,1:T(8,128)} %pad_maximum_fusion, f32[3,1024]{1,0:T(4,128)S(1)} %get-tuple-element.22, f32[3,1024]{1,0:T(4,128)S(1)} %get-tuple-element.23, f32[3,1024]{1,0:T(4,128)S(1)} %get-tuple-element.24, f32[3,1024]{1,0:T(4,128)S(1)} %get-tuple-element.25, ...), kind=kLoop, calls=%fused_computation.10 | loop fusion | flops 25165824 | bytes 47271936 | tf_op jit(solution)/shard_map/convert_element_type | solution.py:100
  169.9 3.6 %slice_bitcast_fusion.1 = (bf16[512,1024]{1,0:T(8,128)(2,1)}, bf16[512,1024]{1,0:T(8,128)(2,1)}, bf16[512,1024]{1,0:T(8,128)(2,1)}) fusion(bf16[512,3,1024]{2,0,1:T(8,128)(2,1)} %fusion.3), kind=kLoop, calls=%fused_computation.38 | loop fusion | bytes 6291456 | tf_op jit(solution)/shard_map/squeeze | solution.py:112
  173.9 152.1 %reduce-scatter.5.cloned.1.call-done = bf16[1024,512]{1,0:T(8,128)(2,1)} async-done(((bf16[1024,4096]{1,0:T(8,128)(2,1)}), bf16[1024,512]{1,0:T(8,128)(2,1)}) %reduce-scatter.5.cloned.1.call-update) | async-done | bytes 1048592 | tf_op jit(solution)/shard_map/reduce_scatter | solution.py:109
  (44 shorter events, 2.5 us)
Async XLA Ops:
  7.2 52.9 %copy-start = (bf16[64,128]{1,0:T(8,128)(2,1)S(1)}, bf16[64,128]{1,0:T(8,128)(2,1)}, u32[]{:S(2)}) copy-start(bf16[64,128]{1,0:T(8,128)(2,1)} %param.11) | copy-start | bytes 49156
  7.2 9.8 %copy-start.6 = (bf16[512,1024]{1,0:T(8,128)(2,1)S(1)}, bf16[512,1024]{1,0:T(8,128)(2,1)}, u32[]{:S(2)}) copy-start(bf16[512,1024]{1,0:T(8,128)(2,1)} %param.9) | copy-start | bytes 3145732
  7.2 9.8 %copy-start.7 = (bf16[512,1024]{1,0:T(8,128)(2,1)S(1)}, bf16[512,1024]{1,0:T(8,128)(2,1)}, u32[]{:S(2)}) copy-start(bf16[512,1024]{1,0:T(8,128)(2,1)} %param.8) | copy-start | bytes 3145732
  7.2 9.8 %copy-start.8 = (bf16[512,1024]{1,0:T(8,128)(2,1)S(1)}, bf16[512,1024]{1,0:T(8,128)(2,1)}, u32[]{:S(2)}) copy-start(bf16[512,1024]{1,0:T(8,128)(2,1)} %param.7) | copy-start | bytes 3145732
  7.2 8.1 %copy-start.10 = (f32[7,3,1024]{2,0,1:T(8,128)S(1)}, f32[7,3,1024]{2,0,1:T(8,128)}, u32[]{:S(2)}) copy-start(f32[7,3,1024]{2,0,1:T(8,128)} %param.10) | copy-start | bytes 258052
  7.2 39.6 %all-gather.2.cloned.1.call-start = ((), (), s32[]{:S(2)}) async-start(), calls=%async_computation.3 | async-start | bytes 5242880 | tf_op jit(solution)/shard_map/all_gather | solution.py:84
  8.0 166.0 %reduce-scatter.3.cloned.1.call-start = ((), (), s32[]{:S(2)}) async-start(), calls=%async_computation.2 | async-start | bytes 5242880 | tf_op jit(solution)/shard_map/reduce_scatter | solution.py:78
  10.4 6.6 %collective-permute-start = (bf16[6,3,1024]{2,0,1:T(8,128)(2,1)S(1)}, bf16[6,3,1024]{2,0,1:T(8,128)(2,1)S(1)}, u32[]{:S(2)}, u32[]{:S(2)}) collective-permute-start(bf16[6,3,1024]{2,0,1:T(8,128)(2,1)S(1)} %slice.138), channel_id=1, source_target_pairs={{0,4},{4,8},{8,12},{12,16},{16,20},{20,24},{24,28},{1,5},{5,9},{9,... | collective-permute-start | bytes 110600 | tf_op jit(solution)/shard_map/ppermute | solution.py:10
  24.5 35.6 %copy-start.9 = (s32[32768]{0:T(1024)S(1)}, s32[32768]{0:T(1024)}, u32[]{:S(2)}) copy-start(s32[32768]{0:T(1024)} %subtract_bitcast_fusion) | copy-start | bytes 393220
  58.6 10.5 %collective-permute-start.2 = (bf16[128,1024]{1,0:T(8,128)(2,1)}, bf16[128,1024]{1,0:T(8,128)(2,1)S(1)}, u32[]{:S(2)}, u32[]{:S(2)}) collective-permute-start(bf16[128,1024]{1,0:T(8,128)(2,1)} %slice.149), channel_id=1, source_target_pairs={{4,0},{8,4},{12,8},{16,12},{20,16},{24,20},{28,24},{5,1},{9,5},{13... | collective-permute-start | bytes 786440 | tf_op jit(solution)/shard_map/ppermute | solution.py:10
  70.1 2.2 copy-start.4
  84.8 17.4 %collective-permute-start.1 = (bf16[128,1024]{1,0:T(8,128)(2,1)}, bf16[128,1024]{1,0:T(8,128)(2,1)S(1)}, u32[]{:S(2)}, u32[]{:S(2)}) collective-permute-start(bf16[128,1024]{1,0:T(8,128)(2,1)} %slice_bitcast_fusion.4), channel_id=1, source_target_pairs={{0,4},{4,8},{8,12},{12,16},{16,20},{20,24},{24,28},{1,5},{5,9},{9,... | collective-permute-start | bytes 786440 | tf_op jit(solution)/shard_map/ppermute | solution.py:10
  105.9 3.2 copy-start.5
  129.9 196.1 %reduce-scatter.5.cloned.1.call-start = ((), (), s32[]{:S(2)}) async-start(), calls=%async_computation.4 | async-start | bytes 9437184 | tf_op jit(solution)/shard_map/reduce_scatter | solution.py:109
  139.4 9.2 %copy-start.2 = (f32[512,1,1024]{2,0,1:T(8,128)S(1)}, f32[512,1,1024]{2,0,1:T(8,128)}, u32[]{:S(2)}) copy-start(f32[512,1,1024]{2,0,1:T(8,128)} %get-tuple-element.6) | copy-start | bytes 6291460
  139.4 9.2 %copy-start.3 = (f32[512,1,1024]{2,0,1:T(8,128)S(1)}, f32[512,1,1024]{2,0,1:T(8,128)}, u32[]{:S(2)}) copy-start(f32[512,1,1024]{2,0,1:T(8,128)} %get-tuple-element.11) | copy-start | bytes 6291460
  142.5 6.0 %collective-permute-start.3 = (bf16[6,3,1024]{2,0,1:T(8,128)(2,1)S(1)}, bf16[6,3,1024]{2,0,1:T(8,128)(2,1)S(1)}, u32[]{:S(2)}, u32[]{:S(2)}) collective-permute-start(bf16[6,3,1024]{2,0,1:T(8,128)(2,1)S(1)} %slice.210), channel_id=1, source_target_pairs={{4,0},{8,4},{12,8},{16,12},{20,16},{24,20},{28,24},{5,1},{9,5},{13... | collective-permute-start | bytes 110600 | tf_op jit(solution)/shard_map/ppermute | solution.py:10
  151.7 174.4 %copy-start.1 = (bf16[64,128]{1,0:T(8,128)(2,1)S(1)}, bf16[64,128]{1,0:T(8,128)(2,1)}, u32[]{:S(2)}) copy-start(bf16[64,128]{1,0:T(8,128)(2,1)} %param.11) | copy-start | bytes 49156
Sparse Core Ops, SparseCore 0:
  9.6 37.1 all-gather.1
  130.0 43.8 reduce-scatter.2
  178.1 147.8 reduce-scatter.4
